TPU v7x, 512 devices: a whole 4x8x8 slice. The times are simulated.
512 devices in a mesh: seq: 64 (over y, x, core), ch: 8 (over z).
Axes of the slice: x: 4, y: 8, z: 8, core: 2. Of those that a mesh axis runs over, the one named last changes fastest.
Arguments:
- signal: bfloat16 [1536, 32768], P('ch', 'seq'), may hold values from -16 to 16
- input_norm_gain: float32 [1536], P('ch'), may hold values from 0.25 to 1.75
- value_weight: bfloat16 [1536, 1536], P('seq', 'ch'), may hold values from -0.15625 to 0.15625
- gate_weight: bfloat16 [1536, 1536], P('seq', 'ch'), may hold values from -0.15625 to 0.15625
- depth_taps: float32 [31, 1536], P(None, 'ch'), may hold values from -1 to 1
- cotangent: bfloat16 [1536, 32768], P('ch', 'seq'), may hold values from -6 to 6
Outputs:
- output: bfloat16 [1536, 32768], P('ch', 'seq')
- signal_gradient: bfloat16 [1536, 32768], P('ch', 'seq')
- grad_value: float32 [1536, 1536], P('seq', 'ch')
- grad_gate: float32 [1536, 1536], P('seq', 'ch')
- grad_taps: float32 [31, 1536], P(None, 'ch')
- gain_gradient: float32 [1536], P('ch')
All inputs are finite; a program needn't handle non-finite values.
Results may differ from a plain program's by a relative error of at most 0.02.
Values may be sent and summed in bfloat16 or wider, within the bound.
No kernel may reach another device: no remote copies, remote signals or barrier semaphores. Data moves between devices by JAX's collectives and lax.ppermute only.
A program may use at most 64 MiB of HBM per device.

v0:
```python
import jax
import jax.numpy as jnp
from jax import lax
from jax.sharding import PartitionSpec as P


def extended(cells, sides, width):
    for axis, dim in sides:
        count = lax.axis_size(axis)
        ends = count - 1
        head = lax.slice_in_dim(cells, 0, width, axis=dim)
        tail = lax.slice_in_dim(cells, cells.shape[dim] - width, cells.shape[dim], axis=dim)
        cells = jnp.concatenate(
            [
                lax.ppermute(tail, axis, [(i, (i + 1) % count) for i in range(ends)]),
                cells,
                lax.ppermute(head, axis, [((i + 1) % count, i) for i in range(ends)]),
            ],
            axis=dim,
        )
    return cells


def standardize_rows(columns_in):
    values = columns_in.astype(jnp.float32)
    average = jnp.mean(values, 0, keepdims=True)
    centred = values - average
    spread = jnp.mean(centred * centred, 0, keepdims=True)
    inverse_deviation = lax.rsqrt(spread + 1e-05)
    return (centred * inverse_deviation, inverse_deviation)


def depthwise(padded, kernel):
    channels = padded.shape[0]
    result = lax.conv_general_dilated(
        padded[None],
        kernel,
        (1,),
        "VALID",
        dimension_numbers=("NCH", "OIH", "NCH"),
        feature_group_count=channels,
        precision=lax.Precision.HIGHEST,
    )
    return result[0]


def shards(signal, input_norm_gain, value_weight, gate_weight, depth_taps, cotangent):
    local_cols = signal.shape[0]
    seq_position = lax.axis_index("seq")
    channel_position = lax.axis_index("ch")
    reach = depth_taps.shape[0] // 2
    complete_signal = lax.all_gather(signal, "ch", axis=0, tiled=True)
    complete_gain = lax.all_gather(input_norm_gain, "ch", axis=0, tiled=True)
    centered_unit, inverse_deviation = standardize_rows(complete_signal)
    normalized_signal = (centered_unit * complete_gain[:, None]).astype(jnp.bfloat16)
    centered_unit_rows = lax.dynamic_slice_in_dim(
        centered_unit, channel_position * local_cols, local_cols, 0
    )
    stacked = jnp.concatenate([value_weight, gate_weight], 1)
    gathered = lax.all_gather(stacked, "seq", axis=0, tiled=True)
    mixed = lax.dot_general(
        gathered, normalized_signal, (((0,), (0,)), ((), ())), preferred_element_type=jnp.float32
    )
    value = mixed[:local_cols]
    gate = mixed[local_cols:]
    sig_gate = jax.nn.sigmoid(gate)
    glued = (value * sig_gate).astype(jnp.bfloat16)
    glued_pad = extended(glued, (("seq", 1),), reach).astype(jnp.float32)
    forward_kernel = depth_taps.T[:, None, :]
    pre = depthwise(glued_pad, forward_kernel)
    sig_pre = jax.nn.sigmoid(pre)
    output = (pre * sig_pre).astype(jnp.bfloat16)
    grad_pre = (cotangent.astype(jnp.float32) * sig_pre * (1.0 + pre * (1.0 - sig_pre))).astype(
        jnp.bfloat16
    )
    grad_pre_f = grad_pre.astype(jnp.float32)
    grad_pad = extended(grad_pre, (("seq", 1),), reach).astype(jnp.float32)
    grad_glued = depthwise(grad_pad, forward_kernel[:, :, ::-1])
    tap_partial = depthwise(glued_pad, grad_pre_f[:, None, :]).T
    grad_v = (grad_glued * sig_gate).astype(jnp.bfloat16)
    grad_g = (grad_glued * value * sig_gate * (1.0 - sig_gate)).astype(jnp.bfloat16)
    grad_both = jnp.concatenate([grad_v, grad_g], 0)
    weight_partial = lax.dot_general(
        normalized_signal, grad_both, (((1,), (1,)), ((), ())), preferred_element_type=jnp.float32
    )
    normed_term = jnp.dot(gathered, grad_both, preferred_element_type=jnp.float32)
    normalized_gradient = lax.psum_scatter(
        normed_term.astype(jnp.bfloat16), "ch", scatter_dimension=0, tiled=True
    ).astype(jnp.float32)
    scaled_signal = normalized_gradient * input_norm_gain[:, None]
    moments = jnp.concatenate(
        [
            jnp.sum(scaled_signal, 0, keepdims=True),
            jnp.sum(scaled_signal * centered_unit_rows, 0, keepdims=True),
        ],
        0,
    )
    moments = lax.psum(moments, "ch") * (1.0 / complete_signal.shape[0])
    inverse_rows = inverse_deviation
    signal_gradient = (
        inverse_rows * (scaled_signal - moments[0:1] - centered_unit_rows * moments[1:2])
    ).astype(jnp.bfloat16)
    gain_portion = jnp.sum(normalized_gradient * centered_unit_rows, 1)
    extra = jnp.concatenate([tap_partial, gain_portion[None]], 0)
    extra = jnp.pad(extra, ((0, 0), (0, weight_partial.shape[1] - extra.shape[1])))
    summed = lax.psum(jnp.concatenate([weight_partial, extra], 0), "seq")
    rows = value_weight.shape[0]
    weight_sums = lax.dynamic_slice_in_dim(summed, seq_position * rows, rows, 0)
    grad_value = weight_sums[:, :local_cols]
    grad_gate = weight_sums[:, local_cols:]
    taps_rows = depth_taps.shape[0]
    full_rows = weight_partial.shape[0]
    grad_taps = summed[full_rows : full_rows + taps_rows, :local_cols]
    gain_gradient = summed[full_rows + taps_rows, :local_cols]
    return (output, signal_gradient, grad_value, grad_gate, grad_taps, gain_gradient)


def solution(mesh):
    placed = (
        P("ch", "seq"),
        P("ch"),
        P("seq", "ch"),
        P("seq", "ch"),
        P(None, "ch"),
        P("ch", "seq"),
    )
    return jax.shard_map(
        shards,
        mesh=mesh,
        in_specs=placed,
        out_specs=(
            P("ch", "seq"),
            P("ch", "seq"),
            P("seq", "ch"),
            P("seq", "ch"),
            P(None, "ch"),
            P("ch"),
        ),
        check_vma=False,
    )
```

profile of v0, /device:TPU:25, one launch (start us, length us, event | category | flops | bytes accessed | tf_op | source)
XLA Modules:
  0.0 444.6 jit_solution(922992032706214905)
XLA Ops:
  7.2 0.7 all-gather.5.cloned.1.call-update
  8.0 1.4 pad_maximum_fusion.5
  9.5 1.3 dynamic-slice
  11.4 0.9 dynamic-update-slice
  12.3 19.7 %all-reduce.1 = f32[1536]{0:T(1024)S(1)} all-reduce(f32[1536]{0:T(1024)S(1)} %dynamic-update-slice), channel_id=1, replica_groups=mesh['seq'=64,'ch'=8] {'ch'}, use_global_device_ids=true, to_apply=%add.1 | all-reduce | flops 1536 | bytes 12288
  32.0 22.1 %all-gather.5.cloned.1.call-done = bf16[1536,512]{1,0:T(8,128)(2,1)} async-done(((bf16[192,512]{1,0:T(8,128)(2,1)}), bf16[1536,512]{1,0:T(8,128)(2,1)}) %all-gather.5.cloned.1.call-update) | async-done | bytes 1572880 | tf_op jit(solution)/shard_map/all_gather | solution.py:52
  54.1 1.8 convert_reduce_fusion
  56.0 0.5 fusion.2
  56.5 84.5 %all-gather.3.cloned.1.call-done = bf16[1536,384]{1,0:T(8,128)(2,1)} async-done(((bf16[24,384]{1,0:T(8,128)(2,1)}), bf16[1536,384]{1,0:T(8,128)(2,1)}) %all-gather.3.cloned.1.call-update) | async-done | bytes 1179664 | tf_op jit(solution)/shard_map/all_gather | solution.py:60
  141.0 2.1 fusion.29
  143.2 0.1 multiply_convert_fusion.5
  143.3 0.1 fusion.46
  143.4 2.2 collective-permute-start.1
  145.5 3.4 collective-permute-start
  149.0 1.1 collective-permute-done
  150.1 0.8 fusion.33
  151.0 0.4 reshape.57
  151.4 0.4 copy.24
  151.9 2.0 convolution_select_fusion.1
  153.9 1.4 copy.36
  155.3 1.0 reshape.55
  156.3 2.0 multiply_convert_fusion.3
  158.4 6.4 %collective-permute-start.3 = (bf16[192,15]{1,0:T(8,128)(2,1)S(1)}, bf16[192,15]{1,0:T(8,128)(2,1)S(1)}, u32[]{:S(2)}, u32[]{:S(2)}) collective-permute-start(bf16[192,15]{1,0:T(8,128)(2,1)S(1)} %get-tuple-element.18), channel_id=1, source_target_pairs={{8,0},{16,8},{24,16},{32,24},{40,32},{48,40},{56,48},{64,56},{72,6... | collective-permute-start | bytes 17288 | tf_op jit(solution)/shard_map/ppermute | solution.py:17
  164.8 1.9 collective-permute-start.2
  166.8 1.2 collective-permute-done.2
  167.9 0.1 maximum_bitcast_fusion
  168.1 0.4 reshape.58
  168.5 0.4 copy.30
  169.0 2.0 convolution_select_fusion
  171.0 1.4 copy.37
  172.4 1.0 reshape.56
  173.5 1.2 multiply_convert_fusion.2
  174.6 3.4 convolution_convert_fusion
  178.1 0.2 all-reduce.4.cloned.1.call-start
  178.3 2.1 fusion
  180.4 0.9 copy.34
  181.3 0.4 copy.35
  181.7 2.2 fusion.48
  184.0 2.4 fusion.28
  186.4 37.6 %reduce-scatter.2.cloned.1.call-done = bf16[192,512]{1,0:T(8,128)(2,1)} async-done(((bf16[1536,512]{1,0:T(8,128)(2,1)}), bf16[192,512]{1,0:T(8,128)(2,1)}) %reduce-scatter.2.cloned.1.call-update) | async-done | bytes 196624 | tf_op jit(solution)/shard_map/reduce_scatter | solution.py:87
  224.0 1.3 fusion.24
  225.3 3.3 pad_maximum_fusion
  228.6 12.6 %psum.14 = f32[2,512]{1,0:T(2,128)S(1)} all-reduce(f32[2,512]{1,0:T(2,128)S(1)} %pad_maximum_fusion.6), channel_id=1, replica_groups=mesh['seq'=64,'ch'=8] {'ch'}, use_global_device_ids=true, to_apply=%region_5.0 | all-reduce | flops 1024 | bytes 8192 | tf_op jit(solution)/shard_map/psum | solution.py:98
  241.2 1.8 fusion.23
  243.0 190.9 %all-reduce.4.cloned.1.call-done = f32[1568,384]{1,0:T(8,128)} async-done(((f32[1568,384]{1,0:T(8,128)}), f32[1568,384]{1,0:T(8,128)}) %all-reduce.4.cloned.1.call-update) | async-done | bytes 2408464 | tf_op jit(solution)/shard_map/psum | solution.py:106
  433.9 1.4 slice.64
  435.3 1.3 slice.65
  436.5 1.5 fusion.44
  (33 shorter events, 0.5 us)
Async XLA Ops:
  7.2 144.7 %copy-start = (f32[31,192]{1,0:T(8,128)S(1)}, f32[31,192]{1,0:T(8,128)}, u32[]{:S(2)}) copy-start(f32[31,192]{1,0:T(8,128)} %param.10) | copy-start | bytes 71428
  7.2 46.9 %all-gather.5.cloned.1.call-start = ((), (), s32[]{:S(2)}) async-start(), calls=%async_computation.2 | async-start | bytes 1769472 | tf_op jit(solution)/shard_map/all_gather | solution.py:52
  7.9 133.1 %all-gather.3.cloned.1.call-start = ((), (), s32[]{:S(2)}) async-start(), calls=%async_computation.1 | async-start | bytes 1198080 | tf_op jit(solution)/shard_map/all_gather | solution.py:60
  9.4 214.6 %reduce-scatter.2.cloned.1.call-start = ((), (), s32[]{:S(2)}) async-start(), calls=%async_computation.3 | async-start | bytes 1769472 | tf_op jit(solution)/shard_map/reduce_scatter | solution.py:87
  54.1 1.9 copy-start.1
  143.2 8.7 %copy-start.5 = (pred[8,68]{0,1:T(8,128)(4,1)S(1)}, pred[8,68]{0,1:T(8,128)(4,1)}, u32[]{:S(2)}) copy-start(pred[8,68]{0,1:T(8,128)(4,1)} %constant.49) | copy-start | bytes 1636
  143.4 5.6 %collective-permute-start.1 = (bf16[192,15]{1,0:T(8,128)(2,1)S(1)}, bf16[192,15]{1,0:T(8,128)(2,1)S(1)}, u32[]{:S(2)}, u32[]{:S(2)}) collective-permute-start(bf16[192,15]{1,0:T(8,128)(2,1)S(1)} %get-tuple-element.20), channel_id=1, source_target_pairs={{8,0},{16,8},{24,16},{32,24},{40,32},{48,40},{56,48},{64,56},{72,6... | collective-permute-start | bytes 17288 | tf_op jit(solution)/shard_map/ppermute | solution.py:17
  145.5 4.6 %collective-permute-start = (bf16[192,15]{1,0:T(8,128)(2,1)S(1)}, bf16[192,15]{1,0:T(8,128)(2,1)S(1)}, u32[]{:S(2)}, u32[]{:S(2)}) collective-permute-start(bf16[192,15]{1,0:T(8,128)(2,1)S(1)} %get-tuple-element.19), channel_id=1, source_target_pairs={{0,8},{8,16},{16,24},{24,32},{32,40},{40,48},{48,56},{56,64},{64,7... | collective-permute-start | bytes 17288 | tf_op jit(solution)/shard_map/ppermute | solution.py:15
  158.4 8.4 %collective-permute-start.3 = (bf16[192,15]{1,0:T(8,128)(2,1)S(1)}, bf16[192,15]{1,0:T(8,128)(2,1)S(1)}, u32[]{:S(2)}, u32[]{:S(2)}) collective-permute-start(bf16[192,15]{1,0:T(8,128)(2,1)S(1)} %get-tuple-element.18), channel_id=1, source_target_pairs={{8,0},{16,8},{24,16},{32,24},{40,32},{48,40},{56,48},{64,56},{72,6... | collective-permute-start | bytes 17288 | tf_op jit(solution)/shard_map/ppermute | solution.py:17
  164.8 3.1 collective-permute-start.2
  178.0 2.4 copy-start.2
  178.1 255.9 %all-reduce.4.cloned.1.call-start = ((), (), s32[]{:S(2)}) async-start(), calls=%async_computation.4 | async-start | bytes 4816896 | tf_op jit(solution)/shard_map/psum | solution.py:106
  184.0 40.0 %copy-start.4 = (f32[192]{0:T(256)S(1)}, f32[192]{0:T(256)}, u32[]{:S(2)}) copy-start(f32[192]{0:T(256)} %param.7) | copy-start | bytes 2308
  228.6 12.6 %copy-start.3 = (bf16[192,512]{1,0:T(8,128)(2,1)S(1)}, bf16[192,512]{1,0:T(8,128)(2,1)}, u32[]{:S(2)}) copy-start(bf16[192,512]{1,0:T(8,128)(2,1)} %reduce-scatter.2.cloned.1.call-done) | copy-start | bytes 589828
Sparse Core Ops, SparseCore 0:
  10.1 43.9 all-gather.4
  57.9 83.0 all-gather.2
  178.2 45.7 reduce-scatter.1
  228.7 205.1 all-reduce.3
where the time goes:
time: 445 us
  waiting for transfers between devices  338 us (76%)
  blocking collectives  32.2 us (7%)
  other arithmetic  16.4 us (4%)
  between operations  14.7 us (3%)
  local copies, waits for them, and re-layouts  14.5 us (3%)
  starting transfers between devices  14.3 us (3%)
  matrix products  14.2 us (3%)
    psum x1, waiting for transfers between devices, shards(): summed = lax.psum(jnp.concatenate([weight_partial, extra], 0), 'seq')  191 us
    all_gather x1, waiting for transfers between devices, shards(): gathered = lax.all_gather(stacked, 'seq', axis=0, tiled=True)  84.5 us
    reduce_scatter x1, waiting for transfers between devices, shards(): lax.psum_scatter(normed_term.astype(jnp.bfloat16), 'ch', scatter_dimensio...  37.6 us
    all_gather x1, waiting for transfers between devices, shards(): complete_signal = lax.all_gather(signal, 'ch', axis=0, tiled=True)  22.1 us
    unnamed x1, blocking collectives  19.7 us
    psum x1, blocking collectives, shards(): moments = lax.psum(moments, 'ch') * (1.0 / complete_signal.shape[0])  12.6 us
  transfers between devices with their start and end apart: 8, of which 6 were waited for; matrix products, arithmetic and copies ran while one was open for 4% of the time, Pallas kernels for 0%

commit v1 on v0

--- a/solution.py
+++ b/solution.py
@@ -2,6 +2,12 @@
 import jax.numpy as jnp
 from jax import lax
 from jax.sharding import PartitionSpec as P
+
+
+def _map_cubes(state, dim_no):
+    shaped = list(state.shape[1:])
+    shaped[dim_no] *= state.shape[0]
+    return jnp.moveaxis(state, 0, dim_no).reshape(shaped)
 
 
 def extended(cells, sides, width):
@@ -49,7 +55,25 @@
     seq_position = lax.axis_index("seq")
     channel_position = lax.axis_index("ch")
     reach = depth_taps.shape[0] // 2
-    complete_signal = lax.all_gather(signal, "ch", axis=0, tiled=True)
+    n_axis = lax.axis_size("ch")
+    line_up = [(h, (h + 1) % n_axis) for h in range(n_axis)]
+    crops = [(c, no) for no, c in line_up]
+    outcome_arr, left_arr = ([], [])
+    for k in range(n_axis - 1):
+        if k % 2 == 0:
+            outcome_arr.append(
+                lax.ppermute(
+                    outcome_arr[-1] if outcome_arr else signal, axis_name="ch", perm=line_up
+                )
+            )
+        else:
+            left_arr.append(
+                lax.ppermute(left_arr[-1] if left_arr else signal, axis_name="ch", perm=crops)
+            )
+    all_values = jnp.stack([*outcome_arr[::-1], signal, *left_arr])
+    heard = lax.axis_index("ch") - len(outcome_arr)
+    all_values = all_values[(jnp.arange(n_axis) - heard) % n_axis]
+    complete_signal = _map_cubes(all_values, 0)
     complete_gain = lax.all_gather(input_norm_gain, "ch", axis=0, tiled=True)
     centered_unit, inverse_deviation = standardize_rows(complete_signal)
     normalized_signal = (centered_unit * complete_gain[:, None]).astype(jnp.bfloat16)

time: 445 us -> 419 us (0.942)
  waiting for transfers between devices: 338 us -> 298 us
  starting transfers between devices: 14.3 us -> 34.7 us
  blocking collectives: 32.2 us -> 26.1 us
    all_gather x1, waiting for transfers between devices: 84.5 us -> 45.6 us  [shards(): gathered = lax.all_gather(stacked, 'seq', axis=0, tiled=True)]
    all_gather x1 -> x0, waiting for transfers between devices: 22.1 us -> none  [shards(): complete_signal = lax.all_gather(signal, 'ch', axis=0, tiled=True)]
    ppermute x0 -> x7, starting transfers between devices: none -> 20.5 us  [the longest x4 11.3 us: shards(): lax.ppermute(outcome_arr[-1] if outcome_arr else signal, axis_name='ch',...]
    ppermute x0 -> x7, waiting for transfers between devices: none -> 20.5 us  [the longest x4 13.3 us: shards(): lax.ppermute(outcome_arr[-1] if outcome_arr else signal, axis_name='ch',...]
    unnamed x1, blocking collectives: 19.7 us -> 13.6 us
  transfers between devices with their start and end apart: 8 -> 14, of which waited for: 6 -> 9; matrix products, arithmetic and copies ran while one was open for 4% -> 4% of each run, Pallas kernels for 0% -> 0%
where the time goes in v1:
time: 419 us; the launch traced here: 418 us
  waiting for transfers between devices  298 us (71%)
  starting transfers between devices  34.7 us (8%)
  blocking collectives  26.1 us (6%)
  local copies, waits for them, and re-layouts  16.1 us (4%)
  other arithmetic  15.1 us (4%)
  between operations  14.8 us (4%)
  matrix products  12.9 us (3%)
    psum x1, waiting for transfers between devices, shards(): summed = lax.psum(jnp.concatenate([weight_partial, extra], 0), 'seq')  191 us
    all_gather x1, waiting for transfers between devices, shards(): gathered = lax.all_gather(stacked, 'seq', axis=0, tiled=True)  45.6 us
    reduce_scatter x1, waiting for transfers between devices, shards(): lax.psum_scatter(normed_term.astype(jnp.bfloat16), 'ch', scatter_dimensio...  39.1 us
    unnamed x1, blocking collectives  13.6 us
    ppermute x4, waiting for transfers between devices, shards(): lax.ppermute(outcome_arr[-1] if outcome_arr else signal, axis_name='ch',...  13.3 us
    psum x1, blocking collectives, shards(): moments = lax.psum(moments, 'ch') * (1.0 / complete_signal.shape[0])  12.5 us
    ppermute x4, starting transfers between devices, shards(): lax.ppermute(outcome_arr[-1] if outcome_arr else signal, axis_name='ch',...  11.3 us
    ppermute x3, starting transfers between devices, shards(): lax.ppermute(left_arr[-1] if left_arr else signal, axis_name='ch', perm=c...  9.21 us
  transfers between devices with their start and end apart: 14, of which 9 were waited for; matrix products, arithmetic and copies ran while one was open for 4% of the time, Pallas kernels for 0%

profile of v1, /device:TPU:25, one launch (start us, length us, event | category | flops | bytes accessed | tf_op | source)
XLA Modules:
  0.0 418.2 jit_solution(9046530505331104461)
XLA Ops:
  7.2 4.1 collective-permute-start
  11.4 11.5 %collective-permute-done = bf16[192,512]{1,0:T(8,128)(2,1)S(1)} collective-permute-done((bf16[192,512]{1,0:T(8,128)(2,1)}, bf16[192,512]{1,0:T(8,128)(2,1)S(1)}, u32[]{:S(2)}, u32[]{:S(2)}) %collective-permute-start) | collective-permute-done | bytes 196640 | tf_op jit(solution)/shard_map/ppermute | solution.py:65
  22.9 1.9 collective-permute-start.1
  24.8 4.6 %collective-permute-start.4 = (bf16[192,512]{1,0:T(8,128)(2,1)}, bf16[192,512]{1,0:T(8,128)(2,1)S(1)}, u32[]{:S(2)}, u32[]{:S(2)}) collective-permute-start(bf16[192,512]{1,0:T(8,128)(2,1)} %param.6), channel_id=1, source_target_pairs={{1,0},{2,1},{3,2},{4,3},{5,4},{6,5},{7,6},{0,7},{9,8},{10,9},{11,1... | collective-permute-start | bytes 589832 | tf_op jit(solution)/shard_map/ppermute | solution.py:71
  29.4 1.8 collective-permute-done.1
  31.1 1.9 collective-permute-start.2
  33.0 1.4 pad_maximum_fusion.5
  34.5 1.3 dynamic-slice
  36.5 0.9 dynamic-update-slice
  37.4 13.6 %all-reduce.1 = f32[1536]{0:T(1024)S(1)} all-reduce(f32[1536]{0:T(1024)S(1)} %dynamic-update-slice), channel_id=1, replica_groups=mesh['seq'=64,'ch'=8] {'ch'}, use_global_device_ids=true, to_apply=%add.1 | all-reduce | flops 1536 | bytes 12288
  51.0 1.9 collective-permute-start.5
  53.0 3.4 collective-permute-start.3
  56.4 1.5 collective-permute-done.5
  57.8 2.7 collective-permute-start.6
  60.8 5.8 %collective-permute-done.6 = bf16[192,512]{1,0:T(8,128)(2,1)S(1)} collective-permute-done((bf16[192,512]{1,0:T(8,128)(2,1)S(1)}, bf16[192,512]{1,0:T(8,128)(2,1)S(1)}, u32[]{:S(2)}, u32[]{:S(2)}) %collective-permute-start.6) | collective-permute-done | bytes 196640 | tf_op jit(solution)/shard_map/ppermute | solution.py:71
  66.5 0.6 gather_fusion
  68.0 2.1 fusion
  70.1 45.6 %all-gather.2.cloned.1.call-done = bf16[1536,384]{1,0:T(8,128)(2,1)} async-done(((bf16[24,384]{1,0:T(8,128)(2,1)}), bf16[1536,384]{1,0:T(8,128)(2,1)}) %all-gather.2.cloned.1.call-update) | async-done | bytes 1179664 | tf_op jit(solution)/shard_map/all_gather | solution.py:84
  115.7 2.1 fusion.48
  118.0 2.2 collective-permute-start.8
  120.2 3.4 collective-permute-start.7
  123.6 1.1 collective-permute-done.7
  124.7 0.8 fusion.30
  126.5 2.0 convolution_select_fusion.1
  128.5 1.4 copy.36
  129.9 1.0 reshape.121
  131.0 2.0 multiply_convert_fusion.3
  133.0 6.4 %collective-permute-start.10 = (bf16[192,15]{1,0:T(8,128)(2,1)S(1)}, bf16[192,15]{1,0:T(8,128)(2,1)S(1)}, u32[]{:S(2)}, u32[]{:S(2)}) collective-permute-start(bf16[192,15]{1,0:T(8,128)(2,1)S(1)} %get-tuple-element.20), channel_id=1, source_target_pairs={{8,0},{16,8},{24,16},{32,24},{40,32},{48,40},{56,48},{64,56},{72,6... | collective-permute-start | bytes 17288 | tf_op jit(solution)/shard_map/ppermute | solution.py:23
  139.5 1.9 collective-permute-start.9
  141.4 1.2 collective-permute-done.9
  143.6 2.0 convolution_select_fusion
  145.7 1.4 copy.37
  147.1 1.0 reshape.122
  148.1 1.3 multiply_convert_fusion.2
  149.5 2.1 convolution_convert_fusion
  151.9 0.7 copy-done.2
  152.6 0.9 copy.34
  153.9 2.2 fusion.47
  156.2 2.4 fusion.26
  158.6 39.1 %reduce-scatter.2.cloned.1.call-done = bf16[192,512]{1,0:T(8,128)(2,1)} async-done(((bf16[1536,512]{1,0:T(8,128)(2,1)}), bf16[192,512]{1,0:T(8,128)(2,1)}) %reduce-scatter.2.cloned.1.call-update) | async-done | bytes 196624 | tf_op jit(solution)/shard_map/reduce_scatter | solution.py:111
  197.7 1.3 fusion.22
  198.9 3.3 pad_maximum_fusion
  202.3 12.5 %psum.14 = f32[2,512]{1,0:T(2,128)S(1)} all-reduce(f32[2,512]{1,0:T(2,128)S(1)} %pad_maximum_fusion.6), channel_id=1, replica_groups=mesh['seq'=64,'ch'=8] {'ch'}, use_global_device_ids=true, to_apply=%region_5.6 | all-reduce | flops 1024 | bytes 8192 | tf_op jit(solution)/shard_map/psum | solution.py:122
  214.8 1.8 fusion.21
  216.6 190.9 %all-reduce.4.cloned.1.call-done = f32[1568,384]{1,0:T(8,128)} async-done(((f32[1568,384]{1,0:T(8,128)}), f32[1568,384]{1,0:T(8,128)}) %all-reduce.4.cloned.1.call-update) | async-done | bytes 2408464 | tf_op jit(solution)/shard_map/psum | solution.py:130
  407.5 1.4 slice.66
  408.9 1.3 slice.67
  410.2 1.5 fusion.43
  (57 shorter events, 4.1 us)
Async XLA Ops:
  7.2 119.3 %copy-start = (f32[31,192]{1,0:T(8,128)S(1)}, f32[31,192]{1,0:T(8,128)}, u32[]{:S(2)}) copy-start(f32[31,192]{1,0:T(8,128)} %param.10) | copy-start | bytes 71428
  7.2 53.5 %copy-start.4 = (bf16[192,512]{1,0:T(8,128)(2,1)S(1)}, bf16[192,512]{1,0:T(8,128)(2,1)}, u32[]{:S(2)}) copy-start(bf16[192,512]{1,0:T(8,128)(2,1)} %param.6) | copy-start | bytes 589828
  7.2 108.5 %all-gather.2.cloned.1.call-start = ((), (), s32[]{:S(2)}) async-start(), calls=%async_computation.1 | async-start | bytes 1198080 | tf_op jit(solution)/shard_map/all_gather | solution.py:84
  7.2 15.6 %collective-permute-start = (bf16[192,512]{1,0:T(8,128)(2,1)}, bf16[192,512]{1,0:T(8,128)(2,1)S(1)}, u32[]{:S(2)}, u32[]{:S(2)}) collective-permute-start(bf16[192,512]{1,0:T(8,128)(2,1)} %param.6), channel_id=1, source_target_pairs={{0,1},{1,2},{2,3},{3,4},{4,5},{5,6},{6,7},{7,0},{8,9},{9,10},{10,1... | collective-permute-start | bytes 589832 | tf_op jit(solution)/shard_map/ppermute | solution.py:65
  22.9 8.3 %collective-permute-start.1 = (bf16[192,512]{1,0:T(8,128)(2,1)S(1)}, bf16[192,512]{1,0:T(8,128)(2,1)S(1)}, u32[]{:S(2)}, u32[]{:S(2)}) collective-permute-start(bf16[192,512]{1,0:T(8,128)(2,1)S(1)} %collective-permute-done), channel_id=1, source_target_pairs={{0,1},{1,2},{2,3},{3,4},{4,5},{5,6},{6,7},{7,0},{8,9},{9,10},{10,1... | collective-permute-start | bytes 589832 | tf_op jit(solution)/shard_map/ppermute | solution.py:65
  24.8 26.2 %collective-permute-start.4 = (bf16[192,512]{1,0:T(8,128)(2,1)}, bf16[192,512]{1,0:T(8,128)(2,1)S(1)}, u32[]{:S(2)}, u32[]{:S(2)}) collective-permute-start(bf16[192,512]{1,0:T(8,128)(2,1)} %param.6), channel_id=1, source_target_pairs={{1,0},{2,1},{3,2},{4,3},{5,4},{6,5},{7,6},{0,7},{9,8},{10,9},{11,1... | collective-permute-start | bytes 589832 | tf_op jit(solution)/shard_map/ppermute | solution.py:71
  31.1 21.8 %collective-permute-start.2 = (bf16[192,512]{1,0:T(8,128)(2,1)S(1)}, bf16[192,512]{1,0:T(8,128)(2,1)S(1)}, u32[]{:S(2)}, u32[]{:S(2)}) collective-permute-start(bf16[192,512]{1,0:T(8,128)(2,1)S(1)} %collective-permute-done.1), channel_id=1, source_target_pairs={{0,1},{1,2},{2,3},{3,4},{4,5},{5,6},{6,7},{7,0},{8,9},{9,10},{10,1... | collective-permute-start | bytes 589832 | tf_op jit(solution)/shard_map/ppermute | solution.py:65
  34.5 163.2 %reduce-scatter.2.cloned.1.call-start = ((), (), s32[]{:S(2)}) async-start(), calls=%async_computation.2 | async-start | bytes 1769472 | tf_op jit(solution)/shard_map/reduce_scatter | solution.py:111
  51.0 6.8 %collective-permute-start.5 = (bf16[192,512]{1,0:T(8,128)(2,1)S(1)}, bf16[192,512]{1,0:T(8,128)(2,1)S(1)}, u32[]{:S(2)}, u32[]{:S(2)}) collective-permute-start(bf16[192,512]{1,0:T(8,128)(2,1)S(1)} %collective-permute-done.4), channel_id=1, source_target_pairs={{1,0},{2,1},{3,2},{4,3},{5,4},{6,5},{7,6},{0,7},{9,8},{10,9},{11,1... | collective-permute-start | bytes 589832 | tf_op jit(solution)/shard_map/ppermute | solution.py:71
  53.0 7.6 %collective-permute-start.3 = (bf16[192,512]{1,0:T(8,128)(2,1)S(1)}, bf16[192,512]{1,0:T(8,128)(2,1)S(1)}, u32[]{:S(2)}, u32[]{:S(2)}) collective-permute-start(bf16[192,512]{1,0:T(8,128)(2,1)S(1)} %collective-permute-done.2), channel_id=1, source_target_pairs={{0,1},{1,2},{2,3},{3,4},{4,5},{5,6},{6,7},{7,0},{8,9},{9,10},{10,1... | collective-permute-start | bytes 589832 | tf_op jit(solution)/shard_map/ppermute | solution.py:65
  57.8 8.7 %collective-permute-start.6 = (bf16[192,512]{1,0:T(8,128)(2,1)S(1)}, bf16[192,512]{1,0:T(8,128)(2,1)S(1)}, u32[]{:S(2)}, u32[]{:S(2)}) collective-permute-start(bf16[192,512]{1,0:T(8,128)(2,1)S(1)} %collective-permute-done.5), channel_id=1, source_target_pairs={{1,0},{2,1},{3,2},{4,3},{5,4},{6,5},{7,6},{0,7},{9,8},{10,9},{11,1... | collective-permute-start | bytes 589832 | tf_op jit(solution)/shard_map/ppermute | solution.py:71
  117.9 8.6 %copy-start.6 = (pred[8,68]{0,1:T(8,128)(4,1)S(1)}, pred[8,68]{0,1:T(8,128)(4,1)}, u32[]{:S(2)}) copy-start(pred[8,68]{0,1:T(8,128)(4,1)} %constant.68) | copy-start | bytes 1636
  118.0 5.6 %collective-permute-start.8 = (bf16[192,15]{1,0:T(8,128)(2,1)S(1)}, bf16[192,15]{1,0:T(8,128)(2,1)S(1)}, u32[]{:S(2)}, u32[]{:S(2)}) collective-permute-start(bf16[192,15]{1,0:T(8,128)(2,1)S(1)} %get-tuple-element.22), channel_id=1, source_target_pairs={{8,0},{16,8},{24,16},{32,24},{40,32},{48,40},{56,48},{64,56},{72,6... | collective-permute-start | bytes 17288 | tf_op jit(solution)/shard_map/ppermute | solution.py:23
  120.2 4.6 %collective-permute-start.7 = (bf16[192,15]{1,0:T(8,128)(2,1)S(1)}, bf16[192,15]{1,0:T(8,128)(2,1)S(1)}, u32[]{:S(2)}, u32[]{:S(2)}) collective-permute-start(bf16[192,15]{1,0:T(8,128)(2,1)S(1)} %get-tuple-element.21), channel_id=1, source_target_pairs={{0,8},{8,16},{16,24},{24,32},{32,40},{40,48},{48,56},{56,64},{64,7... | collective-permute-start | bytes 17288 | tf_op jit(solution)/shard_map/ppermute | solution.py:21
  133.0 8.4 %collective-permute-start.10 = (bf16[192,15]{1,0:T(8,128)(2,1)S(1)}, bf16[192,15]{1,0:T(8,128)(2,1)S(1)}, u32[]{:S(2)}, u32[]{:S(2)}) collective-permute-start(bf16[192,15]{1,0:T(8,128)(2,1)S(1)} %get-tuple-element.20), channel_id=1, source_target_pairs={{8,0},{16,8},{24,16},{32,24},{40,32},{48,40},{56,48},{64,56},{72,6... | collective-permute-start | bytes 17288 | tf_op jit(solution)/shard_map/ppermute | solution.py:23
  139.5 3.1 collective-permute-start.9
  148.1 1.4 copy-start.1
  151.7 0.9 copy-start.2
  151.7 255.8 %all-reduce.4.cloned.1.call-start = ((), (), s32[]{:S(2)}) async-start(), calls=%async_computation.3 | async-start | bytes 4816896 | tf_op jit(solution)/shard_map/psum | solution.py:130
  156.2 41.5 %copy-start.5 = (f32[192]{0:T(256)S(1)}, f32[192]{0:T(256)}, u32[]{:S(2)}) copy-start(f32[192]{0:T(256)} %param.7) | copy-start | bytes 2308
  202.3 12.6 %copy-start.3 = (bf16[192,512]{1,0:T(8,128)(2,1)S(1)}, bf16[192,512]{1,0:T(8,128)(2,1)}, u32[]{:S(2)}) copy-start(bf16[192,512]{1,0:T(8,128)(2,1)} %reduce-scatter.2.cloned.1.call-done) | copy-start | bytes 589828
Sparse Core Ops, SparseCore 0:
  34.6 81.0 all-gather.1
  151.8 45.7 reduce-scatter.1
  202.4 205.0 all-reduce.3
